TPU v7x, 512 devices: a whole 4x8x8 slice. The times are simulated.
512 devices in a mesh: segment: 4 (over z_lo), seq: 16 (over z_hi, x, core), mp: 8 (over y).
Axes of the slice: x: 4, y: 8, z: 8 (z_hi: 2, z_lo: 4; z = z_hi * 4 + z_lo), core: 2. Of those that a mesh axis runs over, the one named last changes fastest.
Arguments:
- latents: bfloat16 [4, 16, 256, 4096], P('segment', 'seq', None, 'mp'), may hold values from -6 to 6
- w_qkv: bfloat16 [4, 4096, 3, 4096], P('segment', 'seq', None, 'mp'), may hold values from -1 to 1
- w_out: bfloat16 [4, 4096, 4096], P('segment', 'mp', 'seq'), may hold values from -0.09375 to 0.09375
- mod_shift: float32 [4, 4096], P('segment'), may hold values from -3 to 3
- mod_scale: float32 [4, 4096], P('segment'), may hold values from 0.1 to 1.9
- mod_gate: float32 [4, 4096], P('segment'), may hold values from 0.5 to 1.5
- counts: int32 [4, 16], P('segment'), may hold values from 64 to 256, as said below
Outputs:
- next_latents: bfloat16 [4, 16, 256, 4096], P('segment', 'seq', None, 'mp')
Inputs may be any that keep to these rules, and one draw needn't show every extreme that they name: `counts`: in every section's clip at least one frame has all 256 patch positions valid.
All inputs are finite; a program needn't handle non-finite values.
Results may differ from a plain program's by a relative error of at most 0.01.
Values may be sent and summed in bfloat16 or wider, within the bound.
No kernel may reach another device: no remote copies, remote signals or barrier semaphores. Data moves between devices by JAX's collectives and lax.ppermute only.
A program may use at most 64 MiB of HBM per device.

v0:
```python
import math
import jax
import jax.numpy as jnp
from jax import lax
from jax.sharding import PartitionSpec as P

HD = 128
EPS = 1e-06
NEG_FILL = -1e30


def passed_along(x, axis, by):
    length = lax.axis_size(axis)
    return lax.ppermute(x, axis, [(i, (i + by) % length) for i in range(length)])


def masked_attention(queries, keys_in, values, usable):
    factor = 1.0 / math.sqrt(queries.shape[-1])
    scores = (
        jnp.einsum("...ihe,...jhe->...hij", queries, keys_in, preferred_element_type=jnp.float32)
        * factor
    )
    allowed = usable[..., None, :, None] & usable[..., None, None, :]
    masked = jnp.where(allowed, scores, NEG_FILL)
    highest = jnp.max(masked, axis=-1, keepdims=True)
    raised = jnp.where(allowed, jnp.exp(masked - highest), 0.0)
    spare_one = jnp.where(usable, 0.0, 1.0)[..., None, :, None]
    weights = (raised / (jnp.sum(raised, axis=-1, keepdims=True) + spare_one)).astype(jnp.bfloat16)
    blended = jnp.einsum(
        "...hij,...jhe->...ihe", weights, values, preferred_element_type=jnp.float32
    )
    return blended.astype(jnp.bfloat16)


def relay_features(rows_now):
    return lax.all_to_all(rows_now, "seq", split_axis=0, concat_axis=0, tiled=True)


def pass_onward(rows_now):
    return passed_along(rows_now, "segment", 1)


def on_device(latents, w_qkv, w_out, mod_shift, mod_scale, mod_gate, counts):
    frames = lax.axis_size("seq")
    patches = latents.shape[2]
    narrow = latents.shape[3]
    span = patches // frames
    segment_rows = latents[0, 0]
    gathered = lax.all_gather(latents, "mp", axis=3, tiled=True)[0, 0]
    widened = gathered.astype(jnp.float32)
    average = jnp.mean(widened, axis=-1, keepdims=True)
    centred = widened - average
    variance = jnp.mean(centred * centred, axis=-1, keepdims=True)
    modulated = (centred * lax.rsqrt(variance + EPS) * mod_scale[0] + mod_shift[0]).astype(
        jnp.bfloat16
    )
    columns = w_qkv.shape[2] * w_qkv.shape[3]
    piece = lax.all_gather(w_qkv, "seq", axis=1, tiled=True)
    height = piece.shape[1]
    projected = jnp.dot(
        modulated, piece.reshape(height, columns), preferred_element_type=jnp.float32
    )
    local_heads = w_qkv.shape[3] // HD
    projected = projected.astype(jnp.bfloat16).reshape(patches, 3, local_heads, HD)
    frame_here = lax.axis_index("seq")
    clip_counts = counts[0]
    positions = jnp.arange(frames)

    def spatial(triple):
        count_here = jnp.sum(jnp.where(positions == frame_here, clip_counts, 0))
        usable = jnp.arange(patches) < count_here
        return masked_attention(triple[:, 0], triple[:, 1], triple[:, 2], usable)

    def temporal(triple):
        by_place = triple.reshape(frames, span, 3, local_heads, HD).transpose(1, 0, 2, 3, 4)
        location = frame_here * span + jnp.arange(span)
        usable = location[:, None] < clip_counts[None, :]
        blended = masked_attention(by_place[:, :, 0], by_place[:, :, 1], by_place[:, :, 2], usable)
        return blended.transpose(1, 0, 2, 3).reshape(patches, local_heads, HD)

    attended = lax.cond(lax.axis_index("segment") % 2 == 0, spatial, temporal, projected)
    attended = attended.reshape(patches, local_heads * HD)
    out_whole = lax.all_gather(w_out, "seq", axis=2, tiled=True)[0]
    member = lax.axis_index("mp")
    partials = jnp.dot(attended, out_whole, preferred_element_type=jnp.float32)
    summed = lax.psum_scatter(
        partials.astype(jnp.bfloat16), "mp", scatter_dimension=1, tiled=True
    ).astype(jnp.float32)
    gate_here = lax.dynamic_slice_in_dim(mod_gate[0], member * narrow, narrow)
    updated = (segment_rows.astype(jnp.float32) + gate_here * summed).astype(jnp.bfloat16)
    updated = updated.reshape(frames, span, narrow)
    moved = pass_onward(relay_features(updated))
    return moved.reshape(1, 1, patches, narrow)


def solution(mesh):
    return jax.shard_map(
        on_device,
        mesh=mesh,
        in_specs=(
            P("segment", "seq", None, "mp"),
            P("segment", "seq", None, "mp"),
            P("segment", "mp", "seq"),
            P("segment", None),
            P("segment", None),
            P("segment", None),
            P("segment", None),
        ),
        out_specs=P("segment", "seq", None, "mp"),
        check_vma=False,
    )
```

profile of v0, /device:TPU:1, one launch (start us, length us, event | category | flops | bytes accessed | tf_op | source)
XLA Modules:
  0.0 384.6 jit_solution(8186895898152812026)
XLA Ops:
  6.5 0.0 copy-start
  6.5 0.0 copy-start.5
  6.5 0.0 copy-start.4
  6.5 0.0 all-gather.4.cloned.1.call-start
  6.5 0.7 all-gather.4.cloned.1.call-update
  7.3 0.0 all-gather.6.cloned.1.call-start
  7.3 2.3 copy.18
  9.6 0.0 all-gather.6.cloned.1.call-update
  9.7 0.0 all-gather.8.cloned.1.call-start
  9.7 0.7 all-gather.8.cloned.1.call-update
  10.4 0.0 reduce-scatter.2.cloned.1.call-start
  10.5 43.7 %all-gather.4.cloned.1.call-done = bf16[1,1,256,4096]{3,2,1,0:T(8,128)(2,1)} async-done(((bf16[1,1,256,512]{3,2,1,0:T(8,128)(2,1)}), bf16[1,1,256,4096]{3,2,1,0:T(8,128)(2,1)}) %all-gather.4.cloned.1.call-update) | async-done | bytes 2097168 | tf_op jit(solution)/shard_map/all_gather | solution.py:49
  54.1 0.0 copy-start.1
  54.1 2.1 convert_reduce_fusion
  56.2 2.3 fusion.30
  58.5 157.1 %all-gather.6.cloned.1.call-done = bf16[1,4096,3,512]{1,3,2,0:T(8,128)(2,1)} async-done(((bf16[1,256,3,512]{1,3,2,0:T(8,128)(2,1)}), bf16[1,4096,3,512]{1,3,2,0:T(8,128)(2,1)}) %all-gather.6.cloned.1.call-update) | async-done | bytes 12582928 | tf_op jit(solution)/shard_map/all_gather | solution.py:58
  215.6 0.0 copy-done.5
  215.6 0.0 copy-done.4
  215.6 0.0 copy-done.1
  215.7 0.0 copy-start.3
  215.7 8.2 %convolution_convert_fusion.3 = bf16[256,1536]{1,0:T(8,128)(2,1)S(1)} fusion(bf16[4096,1536]{0,1:T(8,128)(2,1)} %bitcast.96, bf16[1,1,256,4096]{3,2,1,0:T(8,128)(2,1)S(1)} %copy-done.1, f32[4096]{0:T(1024)S(1)} %bitcast.97, f32[4096]{0:T(1024)S(1)} %bitcast.98, f32[256]{0:T(256)S(1)} %add_rsqrt_fusion, f32[256]{0:T(256)S(1)} %broadcast_multiply_fusion), kind=kOutput, calls=%fused_computation.58 | convolution fusion | flops 3227910144 | bytes 15501312 | tf_op jit(solution)/shard_map/dot_general | solution.py:60
  223.9 0.0 copy-done.3
  223.9 3.7 conditional.1
  223.9 0.6 fusion.14
  224.6 0.6 iota_compare_fusion
  225.1 0.1 broadcast_and_fusion.1
  225.2 0.3 copy.19
  225.5 0.6 fusion.40
  226.2 0.6 broadcast_select_fusion.1
  226.7 0.8 convolution_convert_fusion.1
  227.6 0.0 copy-start.2
  227.6 71.0 %all-gather.8.cloned.1.call-done = bf16[1,512,4096]{2,1,0:T(8,128)(2,1)} async-done(((bf16[1,512,256]{2,1,0:T(8,128)(2,1)}), bf16[1,512,4096]{2,1,0:T(8,128)(2,1)}) %all-gather.8.cloned.1.call-update) | async-done | bytes 4194320 | tf_op jit(solution)/shard_map/all_gather | solution.py:83
  298.5 4.8 %convolution_convert_fusion.2 = bf16[256,4096]{1,0:T(8,128)(2,1)} fusion(bf16[256,512]{0,1:T(8,128)(2,1)S(1)} %get-tuple-element.36, bf16[1,512,4096]{2,1,0:T(8,128)(2,1)} %all-gather.8.cloned.1.call-done), kind=kOutput, calls=%fused_computation.49 | convolution fusion | flops 1074790400 | bytes 6553600 | tf_op jit(solution)/shard_map/dot_general | solution.py:85
  303.4 0.0 reduce-scatter.2.cloned.1.call-update
  303.4 0.0 copy-done
  303.4 36.3 %reduce-scatter.2.cloned.1.call-done = bf16[256,512]{1,0:T(8,128)(2,1)} async-done(((bf16[256,4096]{1,0:T(8,128)(2,1)}), bf16[256,512]{1,0:T(8,128)(2,1)}) %reduce-scatter.2.cloned.1.call-update) | async-done | bytes 262160 | tf_op jit(solution)/shard_map/reduce_scatter | solution.py:86
  339.7 0.0 copy-done.2
  339.7 1.0 fusion.38
  340.7 26.0 %all_to_all.5 = bf16[16,16,512]{2,1,0:T(8,128)(2,1)S(1)} all-to-all(bf16[16,16,512]{2,1,0:T(8,128)(2,1)S(1)} %bitcast.84), channel_id=1, replica_groups=mesh['segment'=4,'seq'=16,'mp'=8] {'seq'}, dimensions={0} | all-to-all | bytes 524288 | tf_op jit(solution)/shard_map/all_to_all | solution.py:36
  366.8 5.0 %collective-permute-start = (bf16[16,16,512]{2,1,0:T(8,128)(2,1)S(1)}, bf16[16,16,512]{2,1,0:T(8,128)(2,1)S(1)}, u32[]{:S(2)}, u32[]{:S(2)}) collective-permute-start(bf16[16,16,512]{2,1,0:T(8,128)(2,1)S(1)} %all_to_all.5), channel_id=1, source_target_pairs={{0,128},{128,256},{256,384},{384,0},{1,129},{129,257},{257,385},{3... | collective-permute-start | bytes 786440 | tf_op jit(solution)/shard_map/ppermute | solution.py:14
  371.7 5.6 %collective-permute-done = bf16[16,16,512]{2,1,0:T(8,128)(2,1)S(1)} collective-permute-done((bf16[16,16,512]{2,1,0:T(8,128)(2,1)S(1)}, bf16[16,16,512]{2,1,0:T(8,128)(2,1)S(1)}, u32[]{:S(2)}, u32[]{:S(2)}) %collective-permute-start) | collective-permute-done | bytes 262176 | tf_op jit(solution)/shard_map/ppermute | solution.py:14
  377.4 0.7 copy.32
  (5 shorter events, 0.0 us)
Async XLA Ops:
  6.5 296.9 %copy-start = (f32[1,4096]{1,0:T(1,128)S(1)}, f32[1,4096]{1,0:T(1,128)}, u32[]{:S(2)}) copy-start(f32[1,4096]{1,0:T(1,128)} %param.14) | copy-start | bytes 49156
  6.5 209.1 %copy-start.5 = (f32[1,4096]{1,0:T(1,128)S(1)}, f32[1,4096]{1,0:T(1,128)}, u32[]{:S(2)}) copy-start(f32[1,4096]{1,0:T(1,128)} %param.13) | copy-start | bytes 49156
  6.5 209.1 %copy-start.4 = (f32[1,4096]{1,0:T(1,128)S(1)}, f32[1,4096]{1,0:T(1,128)}, u32[]{:S(2)}) copy-start(f32[1,4096]{1,0:T(1,128)} %param.12) | copy-start | bytes 49156
  6.5 47.6 %all-gather.4.cloned.1.call-start = ((), (), s32[]{:S(2)}) async-start(), calls=%async_computation.2 | async-start | bytes 2359296 | tf_op jit(solution)/shard_map/all_gather | solution.py:49
  7.3 208.4 %all-gather.6.cloned.1.call-start = ((), (), s32[]{:S(2)}) async-start(), calls=%async_computation.3 | async-start | bytes 13369344 | tf_op jit(solution)/shard_map/all_gather | solution.py:58
  9.7 288.9 %all-gather.8.cloned.1.call-start = ((), (), s32[]{:S(2)}) async-start(), calls=%async_computation.4 | async-start | bytes 4456448 | tf_op jit(solution)/shard_map/all_gather | solution.py:83
  10.4 329.3 %reduce-scatter.2.cloned.1.call-start = ((), (), s32[]{:S(2)}) async-start(), calls=%async_computation.5 | async-start | bytes 2359296 | tf_op jit(solution)/shard_map/reduce_scatter | solution.py:86
  54.1 161.5 %copy-start.1 = (bf16[1,1,256,4096]{3,2,1,0:T(8,128)(2,1)S(1)}, bf16[1,1,256,4096]{3,2,1,0:T(8,128)(2,1)}, u32[]{:S(2)}) copy-start(bf16[1,1,256,4096]{3,2,1,0:T(8,128)(2,1)} %all-gather.4.cloned.1.call-done) | copy-start | bytes 6291460
  215.7 8.3 %copy-start.3 = (s32[1,16]{1,0:T(1,128)S(1)}, s32[1,16]{1,0:T(1,128)}, u32[]{:S(2)}) copy-start(s32[1,16]{1,0:T(1,128)} %param.15) | copy-start | bytes 196
  227.6 112.1 %copy-start.2 = (bf16[1,1,256,512]{3,2,1,0:T(8,128)(2,1)S(1)}, bf16[1,1,256,512]{3,2,1,0:T(8,128)(2,1)}, u32[]{:S(2)}) copy-start(bf16[1,1,256,512]{3,2,1,0:T(8,128)(2,1)} %param.9) | copy-start | bytes 786436
  366.8 10.6 %collective-permute-start = (bf16[16,16,512]{2,1,0:T(8,128)(2,1)S(1)}, bf16[16,16,512]{2,1,0:T(8,128)(2,1)S(1)}, u32[]{:S(2)}, u32[]{:S(2)}) collective-permute-start(bf16[16,16,512]{2,1,0:T(8,128)(2,1)S(1)} %all_to_all.5), channel_id=1, source_target_pairs={{0,128},{128,256},{256,384},{384,0},{1,129},{129,257},{257,385},{3... | collective-permute-start | bytes 786440 | tf_op jit(solution)/shard_map/ppermute | solution.py:14
Sparse Core Ops, SparseCore 0:
  9.4 44.6 all-gather.3
  57.3 158.3 all-gather.5
  218.8 79.7 all-gather.7
  303.5 36.1 reduce-scatter.1
where the time goes:
time: 385 us
  waiting for transfers between devices  315 us (82%)
  blocking collectives  26 us (7%)
  matrix products  14.5 us (4%)
  between operations  13.2 us (3%)
  other arithmetic  7.29 us (2%)
  starting transfers between devices  5.07 us (1%)
    all_gather x1, waiting for transfers between devices, on_device(): piece = lax.all_gather(w_qkv, 'seq', axis=1, tiled=True)  157 us
    all_gather x1, waiting for transfers between devices, on_device(): out_whole = lax.all_gather(w_out, 'seq', axis=2, tiled=True)[0]  71 us
    all_gather x1, waiting for transfers between devices, on_device(): gathered = lax.all_gather(latents, 'mp', axis=3, tiled=True)[0, 0]  43.7 us
    reduce_scatter x1, waiting for transfers between devices, on_device(): lax.psum_scatter(partials.astype(jnp.bfloat16), 'mp', scatter_dimension=1...  36.3 us
    all_to_all x1, blocking collectives, relay_features(): lax.all_to_all(rows_now, 'seq', split_axis=0, concat_axis=0, tiled=True)  26 us
    dot_general x1, matrix products, on_device(): jnp.dot(modulated, piece.reshape(height, columns), preferred_element_type...  8.22 us
  transfers between devices with their start and end apart: 5, of which 5 were waited for; matrix products, arithmetic and copies ran while one was open for 5% of the time, Pallas kernels for 0%

commit v1 on v0

--- a/solution.py
+++ b/solution.py
@@ -3,6 +3,7 @@
 import jax.numpy as jnp
 from jax import lax
 from jax.sharding import PartitionSpec as P
+from jax.lax import all_to_all, axis_size
 
 HD = 128
 EPS = 1e-06
@@ -46,7 +47,9 @@
     narrow = latents.shape[3]
     span = patches // frames
     segment_rows = latents[0, 0]
-    gathered = lax.all_gather(latents, "mp", axis=3, tiled=True)[0, 0]
+    gathered = jnp.concatenate(
+        all_to_all(jnp.stack([latents for _ in range(axis_size("mp"))]), "mp", 0, 0), axis=3
+    )[0, 0]
     widened = gathered.astype(jnp.float32)
     average = jnp.mean(widened, axis=-1, keepdims=True)
     centred = widened - average

time: 385 us -> 341 us (0.89)
  waiting for transfers between devices: 315 us -> 259 us
  starting transfers between devices: 5.07 us -> 12.5 us
    all_gather x1, waiting for transfers between devices: 157 us -> 96 us  [on_device(): piece = lax.all_gather(w_qkv, 'seq', axis=1, tiled=True)]
    all_to_all x0 -> x1, waiting for transfers between devices: none -> 49.8 us  [on_device(): all_to_all(jnp.stack([latents for _ in range(axis_size('mp'))]), 'mp', 0, 0)]
    all_gather x1 -> x0, waiting for transfers between devices: 43.7 us -> none  [on_device(): gathered = lax.all_gather(latents, 'mp', axis=3, tiled=True)[0, 0]]
    all_to_all x0 -> x1, starting transfers between devices: none -> 7.64 us  [on_device(): all_to_all(jnp.stack([latents for _ in range(axis_size('mp'))]), 'mp', 0, 0)]
  transfers between devices with their start and end apart: 5 -> 5, of which waited for: 5 -> 5; matrix products, arithmetic and copies ran while one was open for 5% -> 6% of each run, Pallas kernels for 0% -> 0%
where the time goes in v1:
time: 341 us; the launch traced here: 340 us
  waiting for transfers between devices  259 us (76%)
  blocking collectives  26 us (8%)
  matrix products  15 us (4%)
  between operations  13.2 us (4%)
  starting transfers between devices  12.5 us (4%)
  other arithmetic  7.95 us (2%)
  local copies, waits for them, and re-layouts  6.42 us (2%)
    all_gather x1, waiting for transfers between devices, on_device(): piece = lax.all_gather(w_qkv, 'seq', axis=1, tiled=True)  96 us
    all_gather x1, waiting for transfers between devices, on_device(): out_whole = lax.all_gather(w_out, 'seq', axis=2, tiled=True)[0]  70.5 us
    all_to_all x1, waiting for transfers between devices, on_device(): all_to_all(jnp.stack([latents for _ in range(axis_size('mp'))]), 'mp', 0, 0)  49.8 us
    reduce_scatter x1, waiting for transfers between devices, on_device(): lax.psum_scatter(partials.astype(jnp.bfloat16), 'mp', scatter_dimension=1...  36.3 us
    all_to_all x1, blocking collectives, relay_features(): lax.all_to_all(rows_now, 'seq', split_axis=0, concat_axis=0, tiled=True)  26 us
    dot_general x1, matrix products, on_device(): jnp.dot(modulated, piece.reshape(height, columns), preferred_element_type...  8.7 us
    all_to_all x1, starting transfers between devices, on_device(): all_to_all(jnp.stack([latents for _ in range(axis_size('mp'))]), 'mp', 0, 0)  7.64 us
  transfers between devices with their start and end apart: 5, of which 5 were waited for; matrix products, arithmetic and copies ran while one was open for 6% of the time, Pallas kernels for 0%

profile of v1, /device:TPU:1, one launch (start us, length us, event | category | flops | bytes accessed | tf_op | source)
XLA Modules:
  0.0 340.3 jit_solution(16280349817697929757)
XLA Ops:
  6.5 0.0 copy-start
  6.5 0.0 all-gather.3.cloned.1.call-start
  6.5 2.3 copy.30
  8.9 0.0 copy-start.2
  8.9 0.0 copy-start.3
  8.9 0.0 all-gather.3.cloned.1.call-update
  8.9 0.0 all-gather.5.cloned.1.call-start
  8.9 0.7 all-gather.5.cloned.1.call-update
  9.7 1.1 copy.28
  10.7 1.5 stack.2
  12.2 7.6 %all-to-all-start = ((bf16[8,1,1,256,512]{3,4,2,1,0:T(8,128)(2,1)}), bf16[8,1,1,256,512]{3,4,2,1,0:T(8,128)(2,1)S(1)}, u32[]{:S(2)}, u32[]{:S(2)}) async-start(bf16[8,1,1,256,512]{3,4,2,1,0:T(8,128)(2,1)} %stack.2), calls=%async_computation | async-start | bytes 4194304 | tf_op jit(solution)/shard_map/all_to_all | solution.py:51
  19.9 0.0 reduce-scatter.2.cloned.1.call-start
  19.9 0.5 broadcast.210
  20.4 0.0 copy-done.2
  20.4 0.6 reduce.10
  21.1 0.0 copy-done.3
  21.1 0.6 reduce.11
  21.7 49.8 %all-to-all-done = bf16[8,1,1,256,512]{3,4,2,1,0:T(8,128)(2,1)S(1)} async-done(((bf16[8,1,1,256,512]{3,4,2,1,0:T(8,128)(2,1)}), bf16[8,1,1,256,512]{3,4,2,1,0:T(8,128)(2,1)S(1)}, u32[]{:S(2)}, u32[]{:S(2)}) %all-to-all-start) | async-done | bytes 2097184 | tf_op jit(solution)/shard_map/all_to_all | solution.py:51
  71.5 0.6 convert_reduce_fusion
  72.1 0.6 fusion.26
  72.7 2.7 fusion.29
  75.4 96.0 %all-gather.3.cloned.1.call-done = bf16[1,4096,3,512]{1,3,2,0:T(8,128)(2,1)} async-done(((bf16[1,256,3,512]{1,3,2,0:T(8,128)(2,1)}), bf16[1,4096,3,512]{1,3,2,0:T(8,128)(2,1)}) %all-gather.3.cloned.1.call-update) | async-done | bytes 12582928 | tf_op jit(solution)/shard_map/all_gather | solution.py:61
  171.4 0.0 copy-start.4
  171.4 8.7 %convolution_convert_fusion.3 = bf16[256,1536]{1,0:T(8,128)(2,1)S(1)} fusion(bf16[256,4096]{0,1:T(8,128)(2,1)} %bitcast.78, bf16[4096,1536]{0,1:T(8,128)(2,1)} %bitcast.92), kind=kOutput, calls=%fused_computation.56 | convolution fusion | flops 3221618688 | bytes 15466496 | tf_op jit(solution)/shard_map/dot_general | solution.py:63
  180.1 0.0 copy-done.4
  180.1 3.7 %conditional.1 = (bf16[256,512]{0,1:T(8,128)(2,1)S(1)}) conditional(s32[]{:T(128)} %convert_element_type.51, (s32[]{:T(128)}, s32[1,16]{1,0:T(1,128)S(1)}, bf16[256,1536]{1,0:T(8,128)(2,1)S(1)}) %tuple.25, (s32[]{:T(128)}, s32[16]{0:T(128)S(1)}, s32[1,16]{1,0:T(1,128)S(1)}, bf16[256,1536]{1,0:T(8,128)(2,1)S(1)}) %tuple.26), branch_computations={%region_2.5_spmd, %region_5.9_spmd} | conditional | flops 204410160 | bytes 6552408 | solution.py:84
  180.1 0.6 fusion.14
  180.8 0.6 iota_compare_fusion
  181.3 0.1 broadcast_and_fusion.1
  181.4 0.3 copy.31
  181.7 0.6 fusion.32
  182.4 0.6 broadcast_select_fusion.1
  183.0 0.8 convolution_convert_fusion.1
  183.8 0.0 copy-start.1
  183.8 70.5 %all-gather.5.cloned.1.call-done = bf16[1,512,4096]{2,1,0:T(8,128)(2,1)} async-done(((bf16[1,512,256]{2,1,0:T(8,128)(2,1)}), bf16[1,512,4096]{2,1,0:T(8,128)(2,1)}) %all-gather.5.cloned.1.call-update) | async-done | bytes 4194320 | tf_op jit(solution)/shard_map/all_gather | solution.py:86
  254.3 4.8 %convolution_convert_fusion.2 = bf16[256,4096]{1,0:T(8,128)(2,1)} fusion(bf16[256,512]{0,1:T(8,128)(2,1)S(1)} %get-tuple-element.40, bf16[1,512,4096]{2,1,0:T(8,128)(2,1)} %all-gather.5.cloned.1.call-done), kind=kOutput, calls=%fused_computation.48 | convolution fusion | flops 1074790400 | bytes 6553600 | tf_op jit(solution)/shard_map/dot_general | solution.py:88
  259.1 0.0 reduce-scatter.2.cloned.1.call-update
  259.1 0.0 copy-done
  259.2 36.3 %reduce-scatter.2.cloned.1.call-done = bf16[256,512]{1,0:T(8,128)(2,1)} async-done(((bf16[256,4096]{1,0:T(8,128)(2,1)}), bf16[256,512]{1,0:T(8,128)(2,1)}) %reduce-scatter.2.cloned.1.call-update) | async-done | bytes 262160 | tf_op jit(solution)/shard_map/reduce_scatter | solution.py:89
  295.4 0.0 copy-done.1
  295.4 1.0 add_convert_fusion
  296.5 26.0 %all_to_all.10 = bf16[16,16,512]{2,1,0:T(8,128)(2,1)S(1)} all-to-all(bf16[16,16,512]{2,1,0:T(8,128)(2,1)S(1)} %bitcast.80), channel_id=1, replica_groups=mesh['segment'=4,'seq'=16,'mp'=8] {'seq'}, dimensions={0} | all-to-all | bytes 524288 | tf_op jit(solution)/shard_map/all_to_all | solution.py:37
  322.5 4.8 %collective-permute-start = (bf16[16,16,512]{2,1,0:T(8,128)(2,1)S(1)}, bf16[16,16,512]{2,1,0:T(8,128)(2,1)S(1)}, u32[]{:S(2)}, u32[]{:S(2)}) collective-permute-start(bf16[16,16,512]{2,1,0:T(8,128)(2,1)S(1)} %all_to_all.10), channel_id=1, source_target_pairs={{0,128},{128,256},{256,384},{384,0},{1,129},{129,257},{257,385},{3... | collective-permute-start | bytes 786440 | tf_op jit(solution)/shard_map/ppermute | solution.py:15
  327.3 5.8 %collective-permute-done = bf16[16,16,512]{2,1,0:T(8,128)(2,1)S(1)} collective-permute-done((bf16[16,16,512]{2,1,0:T(8,128)(2,1)S(1)}, bf16[16,16,512]{2,1,0:T(8,128)(2,1)S(1)}, u32[]{:S(2)}, u32[]{:S(2)}) %collective-permute-start) | collective-permute-done | bytes 262176 | tf_op jit(solution)/shard_map/ppermute | solution.py:15
  333.1 0.7 copy.44
  (7 shorter events, 0.0 us)
Async XLA Ops:
  6.5 252.6 %copy-start = (f32[1,4096]{1,0:T(1,128)S(1)}, f32[1,4096]{1,0:T(1,128)}, u32[]{:S(2)}) copy-start(f32[1,4096]{1,0:T(1,128)} %param.14) | copy-start | bytes 49156
  6.5 164.9 %all-gather.3.cloned.1.call-start = ((), (), s32[]{:S(2)}) async-start(), calls=%async_computation.3 | async-start | bytes 13369344 | tf_op jit(solution)/shard_map/all_gather | solution.py:61
  8.9 11.6 %copy-start.2 = (f32[1,4096]{1,0:T(1,128)S(1)}, f32[1,4096]{1,0:T(1,128)}, u32[]{:S(2)}) copy-start(f32[1,4096]{1,0:T(1,128)} %param.12) | copy-start | bytes 49156
  8.9 12.2 %copy-start.3 = (f32[1,4096]{1,0:T(1,128)S(1)}, f32[1,4096]{1,0:T(1,128)}, u32[]{:S(2)}) copy-start(f32[1,4096]{1,0:T(1,128)} %param.13) | copy-start | bytes 49156
  8.9 245.4 %all-gather.5.cloned.1.call-start = ((), (), s32[]{:S(2)}) async-start(), calls=%async_computation.4 | async-start | bytes 4456448 | tf_op jit(solution)/shard_map/all_gather | solution.py:86
  12.2 59.3 %all-to-all-start = ((bf16[8,1,1,256,512]{3,4,2,1,0:T(8,128)(2,1)}), bf16[8,1,1,256,512]{3,4,2,1,0:T(8,128)(2,1)S(1)}, u32[]{:S(2)}, u32[]{:S(2)}) async-start(bf16[8,1,1,256,512]{3,4,2,1,0:T(8,128)(2,1)} %stack.2), calls=%async_computation | async-start | bytes 4194304 | tf_op jit(solution)/shard_map/all_to_all | solution.py:51
  19.9 275.6 %reduce-scatter.2.cloned.1.call-start = ((), (), s32[]{:S(2)}) async-start(), calls=%async_computation.5 | async-start | bytes 2359296 | tf_op jit(solution)/shard_map/reduce_scatter | solution.py:89
  171.4 8.7 %copy-start.4 = (s32[1,16]{1,0:T(1,128)S(1)}, s32[1,16]{1,0:T(1,128)}, u32[]{:S(2)}) copy-start(s32[1,16]{1,0:T(1,128)} %param.15) | copy-start | bytes 196
  183.8 111.7 %copy-start.1 = (bf16[1,1,256,512]{3,2,1,0:T(8,128)(2,1)S(1)}, bf16[1,1,256,512]{3,2,1,0:T(8,128)(2,1)}, u32[]{:S(2)}) copy-start(bf16[1,1,256,512]{3,2,1,0:T(8,128)(2,1)} %param.9) | copy-start | bytes 786436
  322.5 10.6 %collective-permute-start = (bf16[16,16,512]{2,1,0:T(8,128)(2,1)S(1)}, bf16[16,16,512]{2,1,0:T(8,128)(2,1)S(1)}, u32[]{:S(2)}, u32[]{:S(2)}) collective-permute-start(bf16[16,16,512]{2,1,0:T(8,128)(2,1)S(1)} %all_to_all.10), channel_id=1, source_target_pairs={{0,128},{128,256},{256,384},{384,0},{1,129},{129,257},{257,385},{3... | collective-permute-start | bytes 786440 | tf_op jit(solution)/shard_map/ppermute | solution.py:15
Sparse Core Ops, SparseCore 0:
  10.5 160.8 all-gather.2
  174.5 79.7 all-gather.4
  259.2 36.1 reduce-scatter.1
